TPU v7x, 512 devices: a whole 4x4x16 slice. The times are simulated.
512 devices in a mesh: half: 2 (over core), cls: 64 (over z, x), vol: 4 (over y).
Axes of the slice: x: 4, y: 4, z: 16, core: 2. Of those that a mesh axis runs over, the one named last changes fastest.
Arguments:
- images: bfloat16 [16384, 16384], P(('half', 'cls'), 'vol')
- groups: int32 [16384, 1], P(('half', 'cls')), may hold values from 0 to 63; in each aligned block of 128 rows (0 to 127, 128 to 255, ...) at most 4 rows name the same one
- references: bfloat16 [2048, 16384], P('cls', 'vol'), may hold values from -0.046875 to 0.046875
- interp_index: int32 [2048, 16384], P('cls', 'vol'), may hold values from 0 to 2047
- shell_index: int32 [4, 262144], P('vol', ('half', 'cls')), may hold values from 0 to 127
Outputs:
- volume: float32 [4, 262144], P('vol', ('half', 'cls'))
- shell_fsc: float32 [128], replicated
Inputs may be any that keep to these rules, and one draw needn't show every extreme that they name: `groups`: within each aligned block of 128 particles no group appears more than 4 times, a bound that some block reaches.
All inputs are finite; a program needn't handle non-finite values.
Results may differ from a plain program's by a relative error of at most 0.00041.
Values may be sent and summed in bfloat16 or wider, within the bound.
No kernel may reach another device: no remote copies, remote signals or barrier semaphores. Data moves between devices by JAX's collectives and lax.ppermute only.
A program may use at most 64 MiB of HBM per device.

v0:
```python
import jax
import jax.numpy as jnp
from jax import lax
from jax.sharding import PartitionSpec as P

IMG = 128
SHIFTS = 5
NSHELL = 128
PLANES = 4
VBOX = 256
VOXS = 262144
EPS_W = 1e-05
EPS_F = 1e-06


def partner(shard, axis, apart):
    return lax.ppermute(shard, axis, [(i, i ^ 1 << apart) for i in range(lax.axis_size(axis))])


def shards(images, groups, references, interp_index, shell_index):
    n_cls = lax.axis_size("cls")
    n_vol = lax.axis_size("vol")
    n_half = lax.axis_size("half")
    part_count, pix_quarter = images.shape
    class_count = references.shape[0]
    capacity = max(2 * part_count // n_cls, 4)
    slot_count = n_cls * capacity
    owner_ids = groups[:, 0]
    matches = (owner_ids[:, None] == jnp.arange(n_cls, dtype=jnp.int32)[None, :]).astype(jnp.int32)
    order_in = jnp.sum(jnp.cumsum(matches, axis=0) * matches, axis=1) - 1
    slot_ids = owner_ids * capacity + order_in
    slot_hits = slot_ids[None, :] == jnp.arange(slot_count, dtype=jnp.int32)[:, None]
    source_ids = jnp.sum(
        jnp.where(slot_hits, jnp.arange(part_count, dtype=jnp.int32)[None, :], 0), axis=1
    )
    filled = jnp.any(slot_hits, axis=1)
    outgoing = jnp.where(
        filled[:, None], jnp.take(images, source_ids, axis=0), jnp.zeros((), jnp.bfloat16)
    )
    arrived = lax.all_to_all(
        outgoing.reshape(n_cls, capacity, pix_quarter),
        "cls",
        split_axis=0,
        concat_axis=0,
        tiled=True,
    )
    arrived = arrived.reshape(slot_count, pix_quarter)
    quarter_rows = pix_quarter // IMG
    shaped_refs = references.reshape(class_count, quarter_rows, IMG)
    rolled_refs = jnp.concatenate(
        [
            jnp.roll(shaped_refs, -(shift_id - SHIFTS // 2), axis=2).reshape(
                class_count, pix_quarter
            )
            for shift_id in range(SHIFTS)
        ],
        axis=0,
    )
    partial_scores = lax.dot_general(
        arrived, rolled_refs, (((1,), (1,)), ((), ())), preferred_element_type=jnp.float32
    )
    partial_scores = partial_scores.reshape(slot_count, SHIFTS, class_count)
    scores = lax.psum(partial_scores, "vol")
    squares = scores * scores
    mean_square = jnp.mean(squares, axis=(1, 2), keepdims=True)
    weights = (squares / (mean_square + EPS_W)).astype(jnp.bfloat16)
    weighted = lax.dot_general(
        weights.reshape(slot_count, SHIFTS * class_count),
        arrived,
        (((0,), (0,)), ((), ())),
        preferred_element_type=jnp.float32,
    )
    weighted = weighted.reshape(SHIFTS, class_count, quarter_rows, IMG)
    aligned = jnp.roll(weighted[0], -(SHIFTS // 2), axis=2)
    for shift_id in range(1, SHIFTS):
        aligned = aligned + jnp.roll(weighted[shift_id], shift_id - SHIFTS // 2, axis=2)
    column_ids = jnp.arange(pix_quarter, dtype=jnp.int32) % IMG
    placed = interp_index + 2 * VBOX * PLANES * column_ids[None, :]
    slab_part = jax.ops.segment_sum(aligned.reshape(-1), placed.reshape(-1), num_segments=VOXS)
    piece_len = VOXS // (n_half * n_cls)
    slab_part = jnp.transpose(slab_part.reshape(n_half, n_cls, piece_len), (1, 0, 2)).reshape(-1)
    block_len = VOXS // n_cls
    slab_full = lax.psum(slab_part, "cls")
    own_block = lax.dynamic_slice_in_dim(slab_full, lax.axis_index("cls") * block_len, block_len)
    half_id = lax.axis_index("half")
    own_piece = lax.dynamic_slice_in_dim(own_block, half_id * piece_len, piece_len)
    other_piece = lax.dynamic_slice_in_dim(own_block, (1 - half_id) * piece_len, piece_len)
    mirror_piece = partner(other_piece, "half", 0)
    first = jnp.where(half_id == 0, own_piece, mirror_piece)
    second = jnp.where(half_id == 0, mirror_piece, own_piece)
    shell_hot = (shell_index[0][:, None] == jnp.arange(NSHELL, dtype=jnp.int32)[None, :]).astype(
        jnp.float32
    )
    stats = jnp.stack([first * first, second * second, first * second])
    shell_terms = jnp.dot(stats, shell_hot, precision=lax.Precision.HIGHEST)
    shell_sums = lax.psum(shell_terms, ("half", "cls", "vol"))
    shell_fsc = shell_sums[2] / (jnp.sqrt(shell_sums[0]) * jnp.sqrt(shell_sums[1]) + EPS_F)
    mean_sq = (jnp.sum(shell_sums[0]) + jnp.sum(shell_sums[1]) + 2.0 * jnp.sum(shell_sums[2])) / (
        4.0 * n_vol * VOXS
    )
    filter_vox = jnp.dot(shell_hot, shell_fsc, precision=lax.Precision.HIGHEST)
    volume = filter_vox * (0.5 * (first + second)) / jnp.sqrt(mean_sq + EPS_F)
    return (volume[None, :], shell_fsc)


def solution(mesh):
    placed = (
        P(("half", "cls"), "vol"),
        P(("half", "cls"), None),
        P("cls", "vol"),
        P("cls", "vol"),
        P("vol", ("half", "cls")),
    )
    return jax.shard_map(
        shards,
        mesh=mesh,
        in_specs=placed,
        out_specs=(P("vol", ("half", "cls")), P()),
        check_vma=False,
    )
```

profile of v0, /device:TPU:1, one launch (start us, length us, event | category | flops | bytes accessed | tf_op | source)
XLA Modules:
  0.0 1277.2 jit_solution(14044876211775641448)
XLA Ops:
  7.2 0.8 fusion.7
  8.0 0.2 reduce_window_sum.11
  8.2 0.8 select_reduce_fusion.1
  9.0 0.7 add_add_fusion.1
  9.7 0.1 select_reduce_fusion
  9.8 0.1 fusion.6
  9.9 0.1 reduce_sum.60
  10.1 1.8 gather_fusion
  11.9 2.2 gather.7
  14.2 0.1 broadcast_in_dim.51
  14.3 3.7 select_select_fusion
  18.0 19.2 %all-to-all-start = ((bf16[64,4,4096]{2,1,0:T(4,128)(2,1)}), bf16[64,4,4096]{2,1,0:T(4,128)(2,1)S(1)}, u32[]{:S(2)}, u32[]{:S(2)}) async-start(bf16[64,4,4096]{2,1,0:T(4,128)(2,1)} %select_select_fusion), calls=%async_computation | async-start | bytes 4194304 | tf_op jit(solution)/shard_map/all_to_all | solution.py:40
  37.3 0.0 all-reduce.3.cloned.1.call-start
  37.4 0.1 fusion.21
  37.5 0.1 fusion.22
  37.7 0.3 pad_maximum_fusion.2
  38.0 0.1 fusion.23
  38.1 0.1 fusion.24
  38.3 0.3 pad_maximum_fusion.3
  38.6 0.8 bitcast_dynamic-update-slice_fusion.3
  39.4 0.8 bitcast_dynamic-update-slice_fusion.2
  40.2 0.7 constant_dynamic-update-slice_fusion
  40.9 0.8 bitcast_dynamic-update-slice_fusion.1
  41.7 0.8 bitcast_dynamic-update-slice_fusion
  42.5 89.8 %all-to-all-done = bf16[64,4,4096]{2,1,0:T(4,128)(2,1)S(1)} async-done(((bf16[64,4,4096]{2,1,0:T(4,128)(2,1)}), bf16[64,4,4096]{2,1,0:T(4,128)(2,1)S(1)}, u32[]{:S(2)}, u32[]{:S(2)}) %all-to-all-start) | async-done | bytes 2097184 | tf_op jit(solution)/shard_map/all_to_all | solution.py:40
  132.3 2.1 reshape.142
  134.4 3.5 fusion.25
  137.8 0.0 all-reduce.3.cloned.1.call-update
  137.9 0.0 all-reduce.5.cloned.1.call-start
  137.9 1.1 add_bitcast_fusion
  139.0 0.9 copy.9
  139.9 2.1 reshape.116
  142.0 48.2 %all-reduce.3.cloned.1.call-done = f32[256,5,32]{0,2,1:T(8,128)} async-done(((f32[256,5,32]{0,2,1:T(8,128)}), f32[256,5,32]{0,2,1:T(8,128)}) %all-reduce.3.cloned.1.call-update) | async-done | bytes 163856 | tf_op jit(solution)/shard_map/psum | solution.py:63
  190.2 1.0 multiply_reduce_fusion
  191.1 0.9 divide_convert_fusion
  192.1 2.1 fusion.26
  194.2 0.2 slice_bitcast_fusion.2
  194.4 0.1 copy.15
  194.5 0.2 slice.131
  194.7 0.1 copy.16
  194.8 0.2 slice.134
  195.0 0.1 copy.18
  195.1 0.2 slice.138
  195.3 0.1 copy.19
  195.4 0.2 slice.141
  195.6 0.1 copy.17
  195.7 0.2 pad_maximum_fusion
  196.0 0.2 pad_maximum_fusion.1
  196.2 0.3 maximum_add_fusion
  196.5 0.1 add_add_fusion
  196.6 683.3 %scatter_custom_fusion = f32[262144]{0:T(1024)S(1)} fusion(s32[131072]{0:T(1024)} %bitcast.88, f32[131072]{0:T(1024)S(1)} %add_add_fusion, f32[]{:T(128)} %constant.70.clone.1), kind=kCustom, calls=%fused_computation.17 | custom fusion | flops 131072 | bytes 1049088 | tf_op jit(solution)/shard_map/scatter-add | solution.py:79
  879.9 0.2 reshape.123
  880.1 0.8 copy.26
  880.9 1.1 copy.20
  882.1 268.6 %all-reduce.5.cloned.1.call-done = f32[262144]{0:T(1024)} async-done(((f32[262144]{0:T(1024)}), f32[262144]{0:T(1024)}) %all-reduce.5.cloned.1.call-update) | async-done | bytes 1048592 | tf_op jit(solution)/shard_map/psum | solution.py:83
  1150.7 0.8 dynamic_slice.14
  1151.5 12.6 collective-permute-start
  1164.1 0.8 collective-permute-done
  1164.9 0.8 fusion.20
  1165.7 0.6 fusion.1
  1166.2 100.2 %psum.23 = f32[3,128]{1,0:T(4,128)S(1)} all-reduce(f32[3,128]{1,0:T(4,128)S(1)} %fusion.1), channel_id=1, replica_groups=mesh['half'=2,'cls'=64,'vol'=4] {'half','cls','vol'}, use_global_device_ids=true, to_apply=%region_8.9 | all-reduce | flops 384 | bytes 3072 | tf_op jit(solution)/shard_map/psum | solution.py:96
  1266.4 0.7 slice_reduce_fusion.2
  1269.1 0.7 fusion
  1269.8 0.6 multiply_divide_fusion
  (16 shorter events, 0.1 us)
Async XLA Ops:
  7.2 2.9 copy-start
  18.0 19.3 %copy-start.1 = (bf16[32,4096]{1,0:T(8,128)(2,1)S(1)}, bf16[32,4096]{1,0:T(8,128)(2,1)}, u32[]{:S(2)}) copy-start(bf16[32,4096]{1,0:T(8,128)(2,1)} %param.7) | copy-start | bytes 786436
  18.0 114.3 %all-to-all-start = ((bf16[64,4,4096]{2,1,0:T(4,128)(2,1)}), bf16[64,4,4096]{2,1,0:T(4,128)(2,1)S(1)}, u32[]{:S(2)}, u32[]{:S(2)}) async-start(bf16[64,4,4096]{2,1,0:T(4,128)(2,1)} %select_select_fusion), calls=%async_computation | async-start | bytes 4194304 | tf_op jit(solution)/shard_map/all_to_all | solution.py:40
  37.3 152.9 %all-reduce.3.cloned.1.call-start = ((), (), s32[]{:S(2)}) async-start(), calls=%async_computation.1 | async-start | bytes 327680 | tf_op jit(solution)/shard_map/psum | solution.py:63
  137.9 1012.8 %all-reduce.5.cloned.1.call-start = ((), (), s32[]{:S(2)}) async-start(), calls=%async_computation.2 | async-start | bytes 2097152 | tf_op jit(solution)/shard_map/psum | solution.py:83
  880.9 284.8 %copy-start.3 = (s32[1,2048]{1,0:T(1,128)S(1)}, s32[1,2048]{1,0:T(1,128)}, u32[]{:S(2)}) copy-start(s32[1,2048]{1,0:T(1,128)} %param.9) | copy-start | bytes 24580
  1151.5 13.4 %collective-permute-start = (f32[2048]{0:T(1024)S(1)}, f32[2048]{0:T(1024)S(1)}, u32[]{:S(2)}, u32[]{:S(2)}) collective-permute-start(f32[2048]{0:T(1024)S(1)} %dynamic_slice.14), channel_id=1, source_target_pairs={{0,256},{256,0},{1,257},{257,1},{2,258},{258,2},{3,259},{259,3},{4... | collective-permute-start | bytes 24584 | tf_op jit(solution)/shard_map/ppermute | solution.py:17
  1267.1 3.3 copy-start.2
Sparse Core Ops, SparseCore 0:
  138.0 52.1 all-reduce.2
  882.2 268.4 all-reduce.4
where the time goes:
time: 1280 us
  other arithmetic  696 us (54%)
  waiting for transfers between devices  407 us (32%)
  blocking collectives  100 us (8%)
  starting transfers between devices  31.9 us (2%)
  local copies, waits for them, and re-layouts  18.2 us (1%)
  between operations  16.3 us (1%)
    scatter-add x1, other arithmetic, shards(): jax.ops.segment_sum(aligned.reshape(-1), placed.reshape(-1), num_segments...  683 us
    psum x1, waiting for transfers between devices, shards(): slab_full = lax.psum(slab_part, 'cls')  269 us
    psum x1, blocking collectives, shards(): shell_sums = lax.psum(shell_terms, ('half', 'cls', 'vol'))  100 us
    all_to_all x1, waiting for transfers between devices, shards(): lax.all_to_all(outgoing.reshape(n_cls, capacity, pix_quarter), 'cls', spl...  89.8 us
    psum x1, waiting for transfers between devices, shards(): scores = lax.psum(partial_scores, 'vol')  48.2 us
  transfers between devices with their start and end apart: 4, of which 4 were waited for; matrix products, arithmetic and copies ran while one was open for 1% of the time, Pallas kernels for 0%

commit v1 on v0

--- a/solution.py
+++ b/solution.py
@@ -60,7 +60,7 @@
         arrived, rolled_refs, (((1,), (1,)), ((), ())), preferred_element_type=jnp.float32
     )
     partial_scores = partial_scores.reshape(slot_count, SHIFTS, class_count)
-    scores = lax.psum(partial_scores, "vol")
+    scores = jnp.sum(lax.all_gather(partial_scores, "vol"), axis=0)
     squares = scores * scores
     mean_square = jnp.mean(squares, axis=(1, 2), keepdims=True)
     weights = (squares / (mean_square + EPS_W)).astype(jnp.bfloat16)

time: 1280 us -> 1240 us (0.969)
  waiting for transfers between devices: 407 us -> 354 us
    psum x1 -> x0, waiting for transfers between devices: 48.2 us -> none  [shards(): scores = lax.psum(partial_scores, 'vol')]
  transfers between devices with their start and end apart: 4 -> 3, of which waited for: 4 -> 3; matrix products, arithmetic and copies ran while one was open for 1% -> 1% of each run, Pallas kernels for 0% -> 0%
where the time goes in v1:
time: 1240 us
  other arithmetic  696 us (56%)
  waiting for transfers between devices  354 us (29%)
  blocking collectives  112 us (9%)
  starting transfers between devices  31.8 us (3%)
  local copies, waits for them, and re-layouts  20.5 us (2%)
  between operations  16.3 us (1%)
    scatter-add x1, other arithmetic, shards(): jax.ops.segment_sum(aligned.reshape(-1), placed.reshape(-1), num_segments...  683 us
    psum x1, waiting for transfers between devices, shards(): slab_full = lax.psum(slab_part, 'cls')  266 us
    psum x1, blocking collectives, shards(): shell_sums = lax.psum(shell_terms, ('half', 'cls', 'vol'))  100 us
    all_to_all x1, waiting for transfers between devices, shards(): lax.all_to_all(outgoing.reshape(n_cls, capacity, pix_quarter), 'cls', spl...  87.8 us
  transfers between devices with their start and end apart: 3, of which 3 were waited for; matrix products, arithmetic and copies ran while one was open for 1% of the time, Pallas kernels for 0%

profile of v1, /device:TPU:1, one launch (start us, length us, event | category | flops | bytes accessed | tf_op | source)
XLA Modules:
  0.0 1236.8 jit_solution(1766931139198883164)
XLA Ops:
  7.2 0.0 copy-start
  7.2 0.8 fusion.7
  8.0 0.2 reduce_window_sum.11
  8.2 0.8 select_reduce_fusion.1
  9.0 0.7 add_add_fusion.1
  9.7 0.1 select_reduce_fusion
  9.8 0.1 fusion.6
  9.9 0.1 reduce_sum.69
  10.1 1.8 gather_fusion
  11.9 2.2 gather.7
  14.2 0.1 broadcast_in_dim.51
  14.3 3.7 select_select_fusion
  18.0 19.2 %all-to-all-start = ((bf16[64,4,4096]{2,1,0:T(4,128)(2,1)}), bf16[64,4,4096]{2,1,0:T(4,128)(2,1)S(1)}, u32[]{:S(2)}, u32[]{:S(2)}) async-start(bf16[64,4,4096]{2,1,0:T(4,128)(2,1)} %select_select_fusion), calls=%async_computation | async-start | bytes 4194304 | tf_op jit(solution)/shard_map/all_to_all | solution.py:40
  37.3 0.0 all-reduce.2.cloned.1.call-start
  37.4 1.1 add_bitcast_fusion
  38.5 0.9 copy.9
  39.4 0.1 fusion.21
  39.5 0.1 fusion.22
  39.7 0.3 pad_maximum_fusion.2
  40.0 0.1 fusion.23
  40.1 0.1 fusion.24
  40.3 0.3 pad_maximum_fusion.3
  40.6 0.8 bitcast_dynamic-update-slice_fusion.3
  41.4 0.8 bitcast_dynamic-update-slice_fusion.2
  42.2 0.7 constant_dynamic-update-slice_fusion
  42.9 0.8 bitcast_dynamic-update-slice_fusion.1
  43.7 0.8 bitcast_dynamic-update-slice_fusion
  44.5 87.8 %all-to-all-done = bf16[64,4,4096]{2,1,0:T(4,128)(2,1)S(1)} async-done(((bf16[64,4,4096]{2,1,0:T(4,128)(2,1)}), bf16[64,4,4096]{2,1,0:T(4,128)(2,1)S(1)}, u32[]{:S(2)}, u32[]{:S(2)}) %all-to-all-start) | async-done | bytes 2097184 | tf_op jit(solution)/shard_map/all_to_all | solution.py:40
  132.3 2.1 reshape.169
  134.4 2.8 fusion.25
  137.2 11.4 all-gather
  148.6 2.2 reshape.167
  150.8 1.5 reduce_sum.71
  152.4 2.1 reshape.143
  154.4 2.1 fusion.26
  156.6 0.2 slice_bitcast_fusion.2
  156.8 0.1 copy.15
  156.9 0.2 slice.131
  157.1 0.1 copy.16
  157.2 0.2 slice.134
  157.4 0.1 copy.18
  157.5 0.2 slice.138
  157.7 0.1 copy.19
  157.8 0.2 slice.141
  158.0 0.1 copy.17
  158.1 0.2 pad_maximum_fusion
  158.3 0.2 pad_maximum_fusion.1
  158.5 0.3 maximum_add_fusion
  158.9 0.1 add_add_fusion
  159.0 683.5 %scatter_custom_fusion = f32[262144]{0:T(1024)S(1)} fusion(s32[131072]{0:T(1024)} %bitcast.90, f32[131072]{0:T(1024)S(1)} %add_add_fusion, f32[]{:T(128)} %constant.70.clone.1), kind=kCustom, calls=%fused_computation.17 | custom fusion | flops 131072 | bytes 1049088 | tf_op jit(solution)/shard_map/scatter-add | solution.py:79
  842.5 0.2 reshape.149
  842.6 0.8 copy.26
  843.5 1.1 copy.20
  844.6 0.0 all-reduce.2.cloned.1.call-update
  844.6 265.6 %all-reduce.2.cloned.1.call-done = f32[262144]{0:T(1024)} async-done(((f32[262144]{0:T(1024)}), f32[262144]{0:T(1024)}) %all-reduce.2.cloned.1.call-update) | async-done | bytes 1048592 | tf_op jit(solution)/shard_map/psum | solution.py:83
  1110.2 0.8 dynamic_slice.14
  1111.0 12.6 %collective-permute-start = (f32[2048]{0:T(1024)S(1)}, f32[2048]{0:T(1024)S(1)}, u32[]{:S(2)}, u32[]{:S(2)}) collective-permute-start(f32[2048]{0:T(1024)S(1)} %dynamic_slice.14), channel_id=1, source_target_pairs={{0,256},{256,0},{1,257},{257,1},{2,258},{258,2},{3,259},{259,3},{4... | collective-permute-start | bytes 24584 | tf_op jit(solution)/shard_map/ppermute | solution.py:17
  1123.6 0.8 collective-permute-done
  1124.4 0.8 fusion.20
  1125.2 0.6 fusion.1
  1125.7 100.2 %psum.15 = f32[3,128]{1,0:T(4,128)S(1)} all-reduce(f32[3,128]{1,0:T(4,128)S(1)} %fusion.1), channel_id=1, replica_groups=mesh['half'=2,'cls'=64,'vol'=4] {'half','cls','vol'}, use_global_device_ids=true, to_apply=%region_8.9 | all-reduce | flops 384 | bytes 3072 | tf_op jit(solution)/shard_map/psum | solution.py:96
  1225.9 0.7 slice_reduce_fusion.2
  1228.6 0.7 fusion
  1229.3 0.6 multiply_divide_fusion
  (16 shorter events, 0.2 us)
Async XLA Ops:
  7.2 2.9 copy-start
  18.0 19.3 %copy-start.1 = (bf16[32,4096]{1,0:T(8,128)(2,1)S(1)}, bf16[32,4096]{1,0:T(8,128)(2,1)}, u32[]{:S(2)}) copy-start(bf16[32,4096]{1,0:T(8,128)(2,1)} %param.7) | copy-start | bytes 786436
  18.0 114.3 %all-to-all-start = ((bf16[64,4,4096]{2,1,0:T(4,128)(2,1)}), bf16[64,4,4096]{2,1,0:T(4,128)(2,1)S(1)}, u32[]{:S(2)}, u32[]{:S(2)}) async-start(bf16[64,4,4096]{2,1,0:T(4,128)(2,1)} %select_select_fusion), calls=%async_computation | async-start | bytes 4194304 | tf_op jit(solution)/shard_map/all_to_all | solution.py:40
  37.3 1072.9 %all-reduce.2.cloned.1.call-start = ((), (), s32[]{:S(2)}) async-start(), calls=%async_computation.1 | async-start | bytes 2097152 | tf_op jit(solution)/shard_map/psum | solution.py:83
  843.5 281.7 %copy-start.3 = (s32[1,2048]{1,0:T(1,128)S(1)}, s32[1,2048]{1,0:T(1,128)}, u32[]{:S(2)}) copy-start(s32[1,2048]{1,0:T(1,128)} %param.9) | copy-start | bytes 24580
  1111.0 13.4 %collective-permute-start = (f32[2048]{0:T(1024)S(1)}, f32[2048]{0:T(1024)S(1)}, u32[]{:S(2)}, u32[]{:S(2)}) collective-permute-start(f32[2048]{0:T(1024)S(1)} %dynamic_slice.14), channel_id=1, source_target_pairs={{0,256},{256,0},{1,257},{257,1},{2,258},{258,2},{3,259},{259,3},{4... | collective-permute-start | bytes 24584 | tf_op jit(solution)/shard_map/ppermute | solution.py:17
  1226.6 3.3 copy-start.2
Sparse Core Ops, SparseCore 0:
  844.7 265.4 all-reduce.1
